TPU v7x, 256 devices: a whole 4x4x8 slice. The times are simulated.
256 devices in a mesh: wide: 32 (over x, y, core), blk: 8 (over z).
Axes of the slice: x: 4, y: 4, z: 8, core: 2. Of those that a mesh axis runs over, the one named last changes fastest.
Arguments:
- tokens: bfloat16 [1024, 8192], P('wide', 'blk'), may hold values from -6 to 6
- target: bfloat16 [1024, 8192], P('wide', 'blk'), may hold values from -3 to 3
- probe_vector: float32 [8192], P('blk'), may hold values from -12 to 12
- weight_in: bfloat16 [256, 8, 2, 128, 128], P('wide', 'blk'), may hold values from -0.375 to 0.375
- weight_out: bfloat16 [256, 8, 2, 128, 128], P('wide', 'blk'), may hold values from -0.09375 to 0.09375
- slot_rows: int32 [256, 8, 2], P('wide', 'blk'), may hold values from 0 to 7, as said below
- slot_count: int32 [256, 8], P('wide', 'blk'), may hold values from 0 to 2, as said below
Outputs:
- outputs: bfloat16 [1024, 8192], P('wide', 'blk')
- token_grad: bfloat16 [1024, 8192], P('wide', 'blk')
- grad_in: float32 [256, 8, 2, 128, 128], P('wide', 'blk')
- grad_out: float32 [256, 8, 2, 128, 128], P('wide', 'blk')
Inputs may be any that keep to these rules, and one draw needn't show every extreme that they name: `slot_rows`: the 2 entries of one (j, g) are distinct feature blocks of the row group. `slot_count`: every hidden block column has 2 used slots in at least one row group.
All inputs are finite; a program needn't handle non-finite values.
Results may differ from a plain program's by a relative error of at most 0.033.
Values may be sent and summed in bfloat16 or wider, within the bound.
No kernel may reach another device: no remote copies, remote signals or barrier semaphores. Data moves between devices by JAX's collectives and lax.ppermute only.
A program may use at most 64 MiB of HBM per device.

v0:
```python
import math
import jax
import jax.numpy as jnp
from jax import lax
from jax.sharding import PartitionSpec as P


def activate(value):
    return jax.nn.gelu(value, approximate=True)


def activate_slope(value):
    return jax.jvp(activate, (value,), (jnp.ones_like(value),))[1]


def row_stride(count, limit):
    return math.gcd(count, limit)


def by_blocks(blockfn, row_count, limit):
    stride = row_stride(row_count, limit)
    pieces = lax.map(
        lambda index: blockfn(index * stride, stride),
        jnp.arange(row_count // stride, dtype=jnp.int32),
    )
    return pieces.reshape((row_count,) + pieces.shape[2:])


def pick_rows(activity, row_index, block):
    row_total = activity.shape[0]
    columns, slots = row_index.shape
    blocks = activity.reshape(row_total, activity.shape[1] // block, block)
    return jnp.take(blocks, row_index.reshape(-1), axis=1).reshape(row_total, columns, slots, block)


def body(tokens, target, probe_vector, weight_in, weight_out, slot_rows, slot_count):
    columns, unit, slots, block, width_two = weight_in.shape
    features = tokens.shape[1]
    feature_blocks = features // block
    row_index = slot_rows[:, 0]
    in_use = lax.broadcasted_iota(jnp.int32, (columns, slots), 1) < slot_count[:, 0][:, None]
    mask_low = in_use.astype(jnp.bfloat16)[:, :, None, None]
    mask_full = in_use.astype(jnp.float32)[:, :, None, None]
    tiles_in = weight_in[:, 0] * mask_low
    tiles_out = weight_out[:, 0] * mask_low
    onehot = (
        row_index[:, :, None]
        == lax.broadcasted_iota(jnp.int32, (columns, slots, feature_blocks), 2)
    ).astype(jnp.float32)
    chosen = jnp.take(
        probe_vector.reshape(feature_blocks, block), row_index.reshape(-1), axis=0
    ).reshape(columns, slots, block)
    image_part = jnp.einsum(
        "jsk,jskn->jn", chosen, tiles_in.astype(jnp.float32), precision=lax.Precision.HIGHEST
    )
    image, norm_probe = lax.psum((image_part, jnp.sum(probe_vector * probe_vector)), "blk")
    norm_image = lax.psum(jnp.sum(image * image), "wide")
    spectral = jnp.sqrt(norm_image / norm_probe)
    x_full = lax.all_gather(tokens, "wide", axis=0, tiled=True)
    all_rows = x_full.shape[0]
    block_rows = all_rows // lax.axis_size("blk")
    owned = tokens.shape[0]

    def hidden_block_term(start_row, count):
        picked = pick_rows(lax.dynamic_slice_in_dim(x_full, start_row, count, 0), row_index, block)
        product = jnp.einsum("tjsk,jskn->tjn", picked, tiles_in, preferred_element_type=jnp.float32)
        return product.reshape(count, columns * block)

    hidden_own = (
        lax.psum_scatter(
            by_blocks(hidden_block_term, block_rows * lax.axis_size("blk"), 512).astype(
                jnp.bfloat16
            ),
            "blk",
            scatter_dimension=0,
            tiled=True,
        ).astype(jnp.float32)
        / spectral
    )
    active_own = activate(hidden_own).astype(jnp.bfloat16)
    active_full = lax.all_gather(active_own, "blk", axis=0, tiled=True)

    def output_block_term(start_row, count):
        active = lax.dynamic_slice_in_dim(active_full, start_row, count, 0).reshape(
            count, columns, block
        )
        contrib = jnp.einsum(
            "tjk,jskn->tjsn", active, tiles_out, preferred_element_type=jnp.float32
        )
        return jnp.einsum("tjsn,jsr->trn", contrib, onehot).reshape(count, features)

    outputs = lax.psum_scatter(
        by_blocks(output_block_term, owned * lax.axis_size("wide"), 256).astype(jnp.bfloat16),
        "wide",
        scatter_dimension=0,
        tiled=True,
    )
    residual = (outputs.astype(jnp.float32) - target.astype(jnp.float32)).astype(jnp.bfloat16)
    error_full = lax.all_gather(residual, "wide", axis=0, tiled=True)

    def back_block_term(start_row, count):
        picked = pick_rows(
            lax.dynamic_slice_in_dim(error_full, start_row, count, 0), row_index, block
        )
        product = jnp.einsum(
            "tjsn,jskn->tjk", picked, tiles_out, preferred_element_type=jnp.float32
        )
        return product.reshape(count, columns * block)

    back_own = lax.psum_scatter(
        by_blocks(back_block_term, block_rows * lax.axis_size("blk"), 512).astype(jnp.bfloat16),
        "blk",
        scatter_dimension=0,
        tiled=True,
    ).astype(jnp.float32)
    slope_own = (back_own * activate_slope(hidden_own)).astype(jnp.bfloat16)
    slope_full = lax.all_gather(slope_own, "blk", axis=0, tiled=True)
    stride = row_stride(all_rows, 256)

    def grads_block(index, totals):
        start_row = index * stride
        picked_in = pick_rows(
            lax.dynamic_slice_in_dim(x_full, start_row, stride, 0), row_index, block
        )
        picked_err = pick_rows(
            lax.dynamic_slice_in_dim(error_full, start_row, stride, 0), row_index, block
        )
        slope = lax.dynamic_slice_in_dim(slope_full, start_row, stride, 0).reshape(
            stride, columns, block
        )
        active = lax.dynamic_slice_in_dim(active_full, start_row, stride, 0).reshape(
            stride, columns, block
        )
        part_in = jnp.einsum("tjsk,tjn->jskn", picked_in, slope, preferred_element_type=jnp.float32)
        part_out = jnp.einsum(
            "tjk,tjsn->jskn", active, picked_err, preferred_element_type=jnp.float32
        )
        return (totals[0] + part_in, totals[1] + part_out)

    empty = jnp.zeros((columns, slots, block, block), jnp.float32)
    raw_in, raw_out = lax.fori_loop(0, all_rows // stride, grads_block, (empty, empty))
    raw_in = raw_in * mask_full
    grad_out = raw_out * mask_full
    curvature = lax.psum(jnp.sum(raw_in * tiles_in.astype(jnp.float32)), ("wide", "blk"))
    outer = jnp.einsum("jsk,jn->jskn", chosen, image) * mask_full
    grad_in = raw_in / spectral - curvature / (spectral**3 * norm_probe) * outer

    def input_block_term(start_row, count):
        slope = lax.dynamic_slice_in_dim(slope_full, start_row, count, 0).reshape(
            count, columns, block
        )
        contrib = jnp.einsum("tjn,jskn->tjsk", slope, tiles_in, preferred_element_type=jnp.float32)
        return jnp.einsum("tjsk,jsr->trk", contrib, onehot).reshape(count, features)

    token_grad = (
        lax.psum_scatter(
            by_blocks(input_block_term, owned * lax.axis_size("wide"), 256).astype(jnp.bfloat16),
            "wide",
            scatter_dimension=0,
            tiled=True,
        ).astype(jnp.float32)
        / spectral
    ).astype(jnp.bfloat16)
    return (outputs, token_grad, grad_in[:, None], grad_out[:, None])


def solution(mesh):
    in_specs = (
        P("wide", "blk"),
        P("wide", "blk"),
        P("blk"),
        P("wide", "blk", None, None, None),
        P("wide", "blk", None, None, None),
        P("wide", "blk", None),
        P("wide", "blk"),
    )
    out_specs = (
        P("wide", "blk"),
        P("wide", "blk"),
        P("wide", "blk", None, None, None),
        P("wide", "blk", None, None, None),
    )
    return jax.shard_map(body, mesh=mesh, in_specs=in_specs, out_specs=out_specs, check_vma=False)
```

profile of v0, /device:TPU:1, one launch (start us, length us, event | category | flops | bytes accessed | tf_op | source)
XLA Modules:
  0.0 652.1 jit_solution(13190907771488800029)
XLA Ops:
  9.5 2.1 bitcast_multiply_fusion
  12.7 51.0 %all-gather.5.cloned.1.call-done = bf16[1024,1024]{1,0:T(8,128)(2,1)} async-done(((bf16[32,1024]{1,0:T(8,128)(2,1)}), bf16[1024,1024]{1,0:T(8,128)(2,1)}) %all-gather.5.cloned.1.call-update) | async-done | bytes 2097168 | tf_op jit(solution)/shard_map/all_gather | solution.py:59
  63.7 3.9 copy.95
  69.1 15.2 %while.63 = (s32[]{:T(128)}, bf16[2,512,1024]{1,2,0:T(8,128)(2,1)}, s32[2]{0:T(128)S(1)}, bf16[1024,1024]{0,1:T(8,128)(2,1)}, s32[8,1,2]{2,0,1:T(8,128)}, /*inde...) while((s32[]{:T(128)}, bf16[2,512,1024]{1,2,0:T(8,128)(2,1)}, ...), condition=%wide.wide.region_1.3_spmd, body=%wide.wide.region_0.0_spmd.sunk | while | flops 269485216 | bytes 37229152 | solution.py:22
  84.3 3.9 copy.132
  90.7 15.5 %all-reduce = (f32[8,128]{1,0:T(8,128)S(1)}, f32[]{:T(128)}) all-reduce(f32[8,128]{1,0:T(8,128)S(1)} %bitcast.244, f32[]{:T(128)} %multiply_reduce_fusion.1), channel_id=1, replica_groups=mesh['wide'=32,'blk'=8] {'blk'}, use_global_device_ids=true, to_apply=%region_3.5 | all-reduce | flops 1025 | bytes 8200 | tf_op jit(solution)/shard_map/psum | solution.py:56
  106.8 65.7 %psum.29 = f32[]{:T(128)} all-reduce(f32[]{:T(128)} %multiply_reduce_fusion.2), channel_id=1, replica_groups=mesh['wide'=32,'blk'=8] {'wide'}, use_global_device_ids=true, to_apply=%region_5.7 | all-reduce | flops 1 | bytes 8 | tf_op jit(solution)/shard_map/psum | solution.py:57
  176.0 37.4 %all-gather.7.cloned.1.call-done = bf16[1024,1024]{0,1:T(8,128)(2,1)} async-done(((bf16[128,1024]{0,1:T(8,128)(2,1)}), bf16[1024,1024]{0,1:T(8,128)(2,1)}) %all-gather.7.cloned.1.call-update) | async-done | bytes 2097168 | tf_op jit(solution)/shard_map/all_gather | solution.py:81
  215.0 18.3 %while.61 = (s32[]{:T(128)}, bf16[4,256,1024]{2,1,0:T(8,128)(2,1)}, s32[4]{0:T(128)S(1)}, bf16[1024,1024]{0,1:T(8,128)(2,1)}, bf16[8,2,128,128]{3,2,1,0:T(8,128)...) while((s32[]{:T(128)}, bf16[4,256,1024]{2,1,0:T(8,128)(2,1)}, ...), condition=%wide.region_9.11_spmd.clone, body=%wide.region_8.10_spmd.clone.sunk | while | flops 142606592 | bytes 6816483 | solution.py:22
  233.4 87.8 %reduce-scatter.9.cloned.1.call-done = bf16[32,1024]{1,0:T(8,128)(2,1)} async-done(((bf16[1024,1024]{1,0:T(8,128)(2,1)}), bf16[32,1024]{1,0:T(8,128)(2,1)}) %reduce-scatter.9.cloned.1.call-update) | async-done | bytes 65552 | tf_op jit(solution)/shard_map/reduce_scatter | solution.py:92
  322.9 51.6 %all-gather.9.cloned.1.call-done = bf16[1024,1024]{1,0:T(8,128)(2,1)} async-done(((bf16[32,1024]{1,0:T(8,128)(2,1)}), bf16[1024,1024]{1,0:T(8,128)(2,1)}) %all-gather.9.cloned.1.call-update) | async-done | bytes 2097168 | tf_op jit(solution)/shard_map/all_gather | solution.py:99
  374.5 3.9 copy.101
  380.0 15.5 %while.64 = (s32[]{:T(128)}, bf16[2,512,1024]{1,2,0:T(8,128)(2,1)}, s32[2]{0:T(128)S(1)}, bf16[1024,1024]{0,1:T(8,128)(2,1)}, s32[8,1,2]{2,0,1:T(8,128)}, /*inde...) while((s32[]{:T(128)}, bf16[2,512,1024]{1,2,0:T(8,128)(2,1)}, ...), condition=%wide.wide.region_12.14_spmd, body=%wide.wide.region_11.13_spmd.sunk | while | flops 269485216 | bytes 39326336 | solution.py:22
  395.5 4.0 copy.133
  399.5 37.0 %reduce-scatter.15.cloned.1.call-done = bf16[128,1024]{1,0:T(8,128)(2,1)} async-done(((bf16[1024,1024]{1,0:T(8,128)(2,1)}), bf16[128,1024]{1,0:T(8,128)(2,1)}) %reduce-scatter.15.cloned.1.call-update) | async-done | bytes 262160
  439.1 46.3 %all-gather.11.cloned.1.call-done = bf16[1024,1024]{0,1:T(8,128)(2,1)} async-done(((bf16[128,1024]{0,1:T(8,128)(2,1)}), bf16[1024,1024]{0,1:T(8,128)(2,1)}) %all-gather.11.cloned.1.call-update) | async-done | bytes 2097168 | tf_op jit(solution)/shard_map/all_gather | solution.py:117
  487.1 18.8 %while.62 = (s32[]{:T(128)}, bf16[4,256,1024]{2,1,0:T(8,128)(2,1)}, s32[4]{0:T(128)S(1)}, bf16[1024,1024]{0,1:T(8,128)(2,1)}, bf16[8,2,128,128]{3,2,1,0:T(8,128)...) while((s32[]{:T(128)}, bf16[4,256,1024]{2,1,0:T(8,128)(2,1)}, ...), condition=%wide.region_15.17_spmd.clone, body=%wide.region_14.16_spmd.clone.sunk | while | flops 142606592 | bytes 6816483 | solution.py:22
  505.9 51.6 %while.65 = (s32[]{:T(128)}, f32[8,2,128,128]{3,2,1,0:T(8,128)}, f32[8,2,128,128]{2,3,1,0:T(8,128)}, bf16[1024,1024]{0,1:T(8,128)(2,1)}, s32[8,1,2]{2,0,1:T(8,12...) while((s32[]{:T(128)}, f32[8,2,128,128]{3,2,1,0:T(8,128)}, ...), condition=%wide.wide.region_18.21_spmd.clone, body=%wide.wide.region_17.20_spmd.clone.sunk | while | flops 270533760 | bytes 28316308 | solution.py:141
  506.0 2.1 constant_dynamic-slice_fusion.22
  513.5 2.6 fusion.105
  517.6 2.1 constant_dynamic-slice_fusion.22
  525.2 3.0 fusion.105
  528.2 2.7 convolution_add_fusion.3
  530.9 2.1 constant_dynamic-slice_fusion.22
  538.5 3.0 fusion.105
  541.5 2.7 convolution_add_fusion.3
  544.2 2.1 constant_dynamic-slice_fusion.22
  551.8 3.0 fusion.105
  554.8 2.7 convolution_add_fusion.3
  557.5 2.4 multiply_reduce_fusion
  560.5 79.3 %psum.31 = f32[]{:T(128)} all-reduce(f32[]{:T(128)} %multiply_reduce_fusion), channel_id=1, replica_groups=mesh['wide'=32,'blk'=8] {'wide','blk'}, use_global_device_ids=true, to_apply=%region_20.23 | all-reduce | flops 1 | bytes 8 | tf_op jit(solution)/shard_map/psum | solution.py:144
  640.8 2.9 multiply_bitcast_fusion
  (242 shorter events, 103.2 us)
Async XLA Ops:
  7.2 56.5 %all-gather.5.cloned.1.call-start = ((), (), s32[]{:S(2)}) async-start(), calls=%async_computation.4 | async-start | bytes 2162688 | tf_op jit(solution)/shard_map/all_gather | solution.py:59
  7.9 165.9 %reduce-scatter.13.cloned.1.call-start = ((), (), s32[]{:S(2)}) async-start(), calls=%async_computation.10 | async-start | bytes 2359296
  8.7 58.9 %copy-start.16 = (s32[8,1,2]{2,0,1:T(8,128)}, s32[8,1,2]{2,0,1:T(8,128)S(1)}, u32[]{:S(2)}) copy-start(s32[8,1,2]{2,0,1:T(8,128)S(1)} %copy.96) | copy-start | bytes 196
  11.6 57.5 %copy-start.5 = (bf16[8,2,128,128]{3,2,1,0:T(8,128)(2,1)}, bf16[8,2,128,128]{3,2,1,0:T(8,128)(2,1)S(1)}, u32[]{:S(2)}) copy-start(bf16[8,2,128,128]{3,2,1,0:T(8,128)(2,1)S(1)} %get-tuple-element.952) | copy-start | bytes 1572868
  73.6 1.6 copy-start.10
  81.2 1.6 copy-start.10
  88.2 2.1 copy-start.6
  88.3 126.8 %copy-start.1 = (bf16[8,2,128,128]{3,2,1,0:T(8,128)(2,1)S(1)}, bf16[8,2,128,128]{3,2,1,0:T(8,128)(2,1)}, u32[]{:S(2)}) copy-start(bf16[8,2,128,128]{3,2,1,0:T(8,128)(2,1)} %get-tuple-element.920) | copy-start | bytes 1572868
  88.3 125.1 %all-gather.7.cloned.1.call-start = ((), (), s32[]{:S(2)}) async-start(), calls=%async_computation.5 | async-start | bytes 2359296 | tf_op jit(solution)/shard_map/all_gather | solution.py:81
  175.9 145.3 %reduce-scatter.9.cloned.1.call-start = ((), (), s32[]{:S(2)}) async-start(), calls=%async_computation.6 | async-start | bytes 2162688 | tf_op jit(solution)/shard_map/reduce_scatter | solution.py:92
  233.3 87.9 %copy-start.19 = (bf16[32,1024]{1,0:T(8,128)(2,1)S(1)}, bf16[32,1024]{1,0:T(8,128)(2,1)}, u32[]{:S(2)}) copy-start(bf16[32,1024]{1,0:T(8,128)(2,1)} %param.22) | copy-start | bytes 196612
  233.4 141.2 %all-gather.9.cloned.1.call-start = ((), (), s32[]{:S(2)}) async-start(), calls=%async_computation.7 | async-start | bytes 2162688 | tf_op jit(solution)/shard_map/all_gather | solution.py:99
  322.8 113.8 %reduce-scatter.15.cloned.1.call-start = ((), (), s32[]{:S(2)}) async-start(), calls=%async_computation.11 | async-start | bytes 2359296
  380.0 2.6 copy-start.2
  384.6 1.6 copy-start.12
  386.3 1.4 copy-start.13
  387.7 2.6 copy-start.2
  392.3 1.6 copy-start.12
  394.1 1.4 copy-start.13
  399.5 39.6 %copy-start.18 = (s32[8,1,2]{2,0,1:T(8,128)S(1)}, s32[8,1,2]{2,0,1:T(8,128)}, u32[]{:S(2)}) copy-start(s32[8,1,2]{2,0,1:T(8,128)} %get-tuple-element.1050) | copy-start | bytes 196
  399.5 87.6 %copy-start.7 = (bf16[8,2,128,128]{3,2,1,0:T(8,128)(2,1)S(1)}, bf16[8,2,128,128]{3,2,1,0:T(8,128)(2,1)}, u32[]{:S(2)}) copy-start(bf16[8,2,128,128]{3,2,1,0:T(8,128)(2,1)} %copy-done.5) | copy-start | bytes 1572868
  399.5 86.0 %all-gather.11.cloned.1.call-start = ((), (), s32[]{:S(2)}) async-start(), calls=%async_computation.8 | async-start | bytes 2359296 | tf_op jit(solution)/shard_map/all_gather | solution.py:117
  438.8 204.9 %reduce-scatter.11.cloned.1.call-start = ((), (), s32[]{:S(2)}) async-start(), calls=%async_computation.9 | async-start | bytes 2162688 | tf_op jit(solution)/shard_map/reduce_scatter | solution.py:156
  513.5 2.6 copy-start
  513.5 2.6 copy-start.4
  525.2 3.0 copy-start
  525.2 3.0 copy-start.4
  538.5 3.0 copy-start
  538.5 3.0 copy-start.4
  551.8 3.0 copy-start
  551.8 3.0 copy-start.4
  557.5 82.3 %copy-start.8 = (f32[8,2,128,128]{2,3,1,0:T(8,128)S(1)}, f32[8,2,128,128]{2,3,1,0:T(8,128)}, u32[]{:S(2)}) copy-start(f32[8,2,128,128]{2,3,1,0:T(8,128)} %get-tuple-element.279) | copy-start | bytes 3145732
  (9 other events, 9.2 us)
Sparse Core Ops, SparseCore 0:
  10.6 53.0 all-gather.4
  88.4 37.0 reduce-scatter.12
  176.0 37.3 all-gather.6
  233.5 87.7 reduce-scatter.8
  324.2 50.2 all-gather.8
  399.6 36.9 reduce-scatter.14
  438.9 46.4 all-gather.10
  506.1 87.7 reduce-scatter.10
where the time goes:
time: 654 us; the launch traced here: 652 us
  waiting for transfers between devices  312 us (48%)
  blocking collectives  161 us (25%)
  local copies, waits for them, and re-layouts  98.7 us (15%)
  matrix products  34 us (5%)
  other arithmetic  20.6 us (3%)
  between operations  16.8 us (3%)
  loops' own time  8.79 us (1%)
    reduce_scatter x1, waiting for transfers between devices, body(): lax.psum_scatter(by_blocks(output_block_term, owned * lax.axis_size('wide...  87.8 us
    psum x1, blocking collectives, body(): lax.psum(jnp.sum(raw_in * tiles_in.astype(jnp.float32)), ('wide', 'blk'))  79.3 us
    psum x1, blocking collectives, body(): norm_image = lax.psum(jnp.sum(image * image), 'wide')  65.7 us
    all_gather x1, waiting for transfers between devices, body(): error_full = lax.all_gather(residual, 'wide', axis=0, tiled=True)  51.6 us
    all_gather x1, waiting for transfers between devices, body(): x_full = lax.all_gather(tokens, 'wide', axis=0, tiled=True)  51 us
    all_gather x1, waiting for transfers between devices, body(): slope_full = lax.all_gather(slope_own, 'blk', axis=0, tiled=True)  46.3 us
    unnamed x10, waiting for transfers between devices  37.8 us
    all_gather x1, waiting for transfers between devices, body(): active_full = lax.all_gather(active_own, 'blk', axis=0, tiled=True)  37.4 us
  transfers between devices with their start and end apart: 8, of which 6 were waited for; matrix products, arithmetic and copies ran while one was open for 10% of the time, Pallas kernels for 0%

commit v1 on v0

--- a/solution.py
+++ b/solution.py
@@ -114,7 +114,12 @@
         tiled=True,
     ).astype(jnp.float32)
     slope_own = (back_own * activate_slope(hidden_own)).astype(jnp.bfloat16)
-    slope_full = lax.all_gather(slope_own, "blk", axis=0, tiled=True)
+    ring = [slope_own]
+    for hop in range(7):
+        ring.append(lax.ppermute(ring[-1], "blk", [(dev, (dev + 1) % 8) for dev in range(8)]))
+    slope_full = jnp.roll(
+        jnp.concatenate(ring[::-1], axis=0), (lax.axis_index("blk") + 1) * ring[0].shape[0], axis=0
+    )
     stride = row_stride(all_rows, 256)
 
     def grads_block(index, totals):

time: 654 us -> 668 us (1.021)
  waiting for transfers between devices: 312 us -> 319 us
    ppermute x0 -> x7, waiting for transfers between devices: none -> 53 us  [body(): lax.ppermute(ring[-1], 'blk', [(dev, (dev + 1) % 8) for dev in range(8)])]
    all_gather x1 -> x0, waiting for transfers between devices: 46.3 us -> none  [body(): slope_full = lax.all_gather(slope_own, 'blk', axis=0, tiled=True)]
    unnamed x10 -> x9, waiting for transfers between devices: 37.8 us -> 37.8 us
  transfers between devices with their start and end apart: 8 -> 14, of which waited for: 6 -> 12; matrix products, arithmetic and copies ran while one was open for 10% -> 10% of each run, Pallas kernels for 0% -> 0%
where the time goes in v1:
time: 668 us; the launch traced here: 667 us
  waiting for transfers between devices  319 us (48%)
  blocking collectives  167 us (25%)
  local copies, waits for them, and re-layouts  101 us (15%)
  matrix products  34 us (5%)
  other arithmetic  19.9 us (3%)
  between operations  16.8 us (3%)
  loops' own time  8.34 us (1%)
    reduce_scatter x1, waiting for transfers between devices, body(): lax.psum_scatter(by_blocks(output_block_term, owned * lax.axis_size('wide...  87.8 us
    psum x1, blocking collectives, body(): lax.psum(jnp.sum(raw_in * tiles_in.astype(jnp.float32)), ('wide', 'blk'))  85.6 us
    psum x1, blocking collectives, body(): norm_image = lax.psum(jnp.sum(image * image), 'wide')  65.7 us
    ppermute x7, waiting for transfers between devices, body(): lax.ppermute(ring[-1], 'blk', [(dev, (dev + 1) % 8) for dev in range(8)])  53 us
    all_gather x1, waiting for transfers between devices, body(): error_full = lax.all_gather(residual, 'wide', axis=0, tiled=True)  51.7 us
    all_gather x1, waiting for transfers between devices, body(): x_full = lax.all_gather(tokens, 'wide', axis=0, tiled=True)  51 us
    unnamed x9, waiting for transfers between devices  37.8 us
    all_gather x1, waiting for transfers between devices, body(): active_full = lax.all_gather(active_own, 'blk', axis=0, tiled=True)  37.5 us
  transfers between devices with their start and end apart: 14, of which 12 were waited for; matrix products, arithmetic and copies ran while one was open for 10% of the time, Pallas kernels for 0%

profile of v1, /device:TPU:1, one launch (start us, length us, event | category | flops | bytes accessed | tf_op | source)
XLA Modules:
  0.0 666.5 jit_solution(8611630969942310779)
XLA Ops:
  12.7 51.0 %all-gather.4.cloned.1.call-done = bf16[1024,1024]{1,0:T(8,128)(2,1)} async-done(((bf16[32,1024]{1,0:T(8,128)(2,1)}), bf16[1024,1024]{1,0:T(8,128)(2,1)}) %all-gather.4.cloned.1.call-update) | async-done | bytes 2097168 | tf_op jit(solution)/shard_map/all_gather | solution.py:59
  63.7 3.9 copy.95
  69.1 15.2 %while.63 = (s32[]{:T(128)}, bf16[2,512,1024]{1,2,0:T(8,128)(2,1)}, s32[2]{0:T(128)S(1)}, bf16[1024,1024]{0,1:T(8,128)(2,1)}, s32[8,1,2]{2,0,1:T(8,128)}, /*inde...) while((s32[]{:T(128)}, bf16[2,512,1024]{1,2,0:T(8,128)(2,1)}, ...), condition=%wide.wide.region_1.3_spmd, body=%wide.wide.region_0.0_spmd.sunk | while | flops 269485216 | bytes 37229152 | solution.py:22
  84.3 3.9 copy.132
  90.7 15.5 %all-reduce = (f32[8,128]{1,0:T(8,128)S(1)}, f32[]{:T(128)}) all-reduce(f32[8,128]{1,0:T(8,128)S(1)} %bitcast.244, f32[]{:T(128)} %multiply_reduce_fusion.1), channel_id=1, replica_groups=mesh['wide'=32,'blk'=8] {'blk'}, use_global_device_ids=true, to_apply=%region_3.5 | all-reduce | flops 1025 | bytes 8200 | tf_op jit(solution)/shard_map/psum | solution.py:56
  106.8 65.7 %psum.29 = f32[]{:T(128)} all-reduce(f32[]{:T(128)} %multiply_reduce_fusion.2), channel_id=1, replica_groups=mesh['wide'=32,'blk'=8] {'wide'}, use_global_device_ids=true, to_apply=%region_5.7 | all-reduce | flops 1 | bytes 8 | tf_op jit(solution)/shard_map/psum | solution.py:57
  175.9 37.5 %all-gather.6.cloned.1.call-done = bf16[1024,1024]{0,1:T(8,128)(2,1)} async-done(((bf16[128,1024]{0,1:T(8,128)(2,1)}), bf16[1024,1024]{0,1:T(8,128)(2,1)}) %all-gather.6.cloned.1.call-update) | async-done | bytes 2097168 | tf_op jit(solution)/shard_map/all_gather | solution.py:81
  215.0 18.3 %while.61 = (s32[]{:T(128)}, bf16[4,256,1024]{2,1,0:T(8,128)(2,1)}, s32[4]{0:T(128)S(1)}, bf16[1024,1024]{0,1:T(8,128)(2,1)}, bf16[8,2,128,128]{3,2,1,0:T(8,128)...) while((s32[]{:T(128)}, bf16[4,256,1024]{2,1,0:T(8,128)(2,1)}, ...), condition=%wide.region_9.11_spmd.clone, body=%wide.region_8.10_spmd.clone.sunk | while | flops 142606592 | bytes 6816483 | solution.py:22
  233.4 87.8 %reduce-scatter.9.cloned.1.call-done = bf16[32,1024]{1,0:T(8,128)(2,1)} async-done(((bf16[1024,1024]{1,0:T(8,128)(2,1)}), bf16[32,1024]{1,0:T(8,128)(2,1)}) %reduce-scatter.9.cloned.1.call-update) | async-done | bytes 65552 | tf_op jit(solution)/shard_map/reduce_scatter | solution.py:92
  322.8 51.7 %all-gather.8.cloned.1.call-done = bf16[1024,1024]{1,0:T(8,128)(2,1)} async-done(((bf16[32,1024]{1,0:T(8,128)(2,1)}), bf16[1024,1024]{1,0:T(8,128)(2,1)}) %all-gather.8.cloned.1.call-update) | async-done | bytes 2097168 | tf_op jit(solution)/shard_map/all_gather | solution.py:99
  374.5 3.9 copy.101
  380.0 15.4 %while.64 = (s32[]{:T(128)}, bf16[2,512,1024]{1,2,0:T(8,128)(2,1)}, s32[2]{0:T(128)S(1)}, bf16[1024,1024]{0,1:T(8,128)(2,1)}, s32[8,1,2]{2,0,1:T(8,128)}, /*inde...) while((s32[]{:T(128)}, bf16[2,512,1024]{1,2,0:T(8,128)(2,1)}, ...), condition=%wide.wide.region_12.14_spmd, body=%wide.wide.region_11.13_spmd.sunk | while | flops 269485216 | bytes 39326336 | solution.py:22
  395.4 4.0 copy.133
  399.4 37.0 %reduce-scatter.15.cloned.1.call-done = bf16[128,1024]{1,0:T(8,128)(2,1)} async-done(((bf16[1024,1024]{1,0:T(8,128)(2,1)}), bf16[128,1024]{1,0:T(8,128)(2,1)}) %reduce-scatter.15.cloned.1.call-update) | async-done | bytes 262160
  438.1 6.4 collective-permute-done
  444.5 7.9 %collective-permute-done.1 = bf16[128,1024]{0,1:T(8,128)(2,1)S(1)} collective-permute-done((bf16[128,1024]{0,1:T(8,128)(2,1)S(1)}, bf16[128,1024]{0,1:T(8,128)(2,1)S(1)}, u32[]{:S(2)}, u32[]{:S(2)}) %collective-permute-start.1) | collective-permute-done | bytes 262176 | tf_op jit(solution)/shard_map/ppermute | solution.py:119
  452.4 9.0 %collective-permute-done.2 = bf16[128,1024]{0,1:T(8,128)(2,1)S(1)} collective-permute-done((bf16[128,1024]{0,1:T(8,128)(2,1)S(1)}, bf16[128,1024]{0,1:T(8,128)(2,1)S(1)}, u32[]{:S(2)}, u32[]{:S(2)}) %collective-permute-start.2) | collective-permute-done | bytes 262176 | tf_op jit(solution)/shard_map/ppermute | solution.py:119
  461.4 8.7 %collective-permute-done.3 = bf16[128,1024]{0,1:T(8,128)(2,1)S(1)} collective-permute-done((bf16[128,1024]{0,1:T(8,128)(2,1)S(1)}, bf16[128,1024]{0,1:T(8,128)(2,1)S(1)}, u32[]{:S(2)}, u32[]{:S(2)}) %collective-permute-start.3) | collective-permute-done | bytes 262176 | tf_op jit(solution)/shard_map/ppermute | solution.py:119
  470.1 7.8 %collective-permute-done.4 = bf16[128,1024]{0,1:T(8,128)(2,1)S(1)} collective-permute-done((bf16[128,1024]{0,1:T(8,128)(2,1)S(1)}, bf16[128,1024]{0,1:T(8,128)(2,1)S(1)}, u32[]{:S(2)}, u32[]{:S(2)}) %collective-permute-start.4) | collective-permute-done | bytes 262176 | tf_op jit(solution)/shard_map/ppermute | solution.py:119
  477.9 6.9 %collective-permute-done.5 = bf16[128,1024]{0,1:T(8,128)(2,1)S(1)} collective-permute-done((bf16[128,1024]{0,1:T(8,128)(2,1)S(1)}, bf16[128,1024]{0,1:T(8,128)(2,1)S(1)}, u32[]{:S(2)}, u32[]{:S(2)}) %collective-permute-start.5) | collective-permute-done | bytes 262176 | tf_op jit(solution)/shard_map/ppermute | solution.py:119
  484.8 6.3 collective-permute-done.6
  495.9 18.0 %while.62 = (s32[]{:T(128)}, bf16[4,256,1024]{2,1,0:T(8,128)(2,1)}, s32[4]{0:T(128)S(1)}, bf16[1024,1024]{0,1:T(8,128)(2,1)}, bf16[8,2,128,128]{3,2,1,0:T(8,128)...) while((s32[]{:T(128)}, bf16[4,256,1024]{2,1,0:T(8,128)(2,1)}, ...), condition=%wide.region_15.17_spmd.clone, body=%wide.region_14.16_spmd.clone.sunk | while | flops 142606592 | bytes 6816483 | solution.py:22
  514.0 51.7 %while.65 = (s32[]{:T(128)}, f32[8,2,128,128]{3,2,1,0:T(8,128)}, f32[8,2,128,128]{2,3,1,0:T(8,128)}, bf16[1024,1024]{0,1:T(8,128)(2,1)}, s32[8,1,2]{2,0,1:T(8,12...) while((s32[]{:T(128)}, f32[8,2,128,128]{3,2,1,0:T(8,128)}, ...), condition=%wide.wide.region_18.21_spmd.clone, body=%wide.wide.region_17.20_spmd.clone.sunk | while | flops 270533760 | bytes 28316308 | solution.py:146
  521.6 2.6 fusion.105
  533.3 3.0 fusion.105
  536.3 2.7 convolution_add_fusion.3
  546.6 3.0 fusion.105
  549.6 2.7 convolution_add_fusion.3
  560.0 3.0 fusion.105
  563.0 2.7 convolution_add_fusion.3
  568.6 85.6 %psum.31 = f32[]{:T(128)} all-reduce(f32[]{:T(128)} %multiply_reduce_fusion), channel_id=1, replica_groups=mesh['wide'=32,'blk'=8] {'wide','blk'}, use_global_device_ids=true, to_apply=%region_20.23 | all-reduce | flops 1 | bytes 8 | tf_op jit(solution)/shard_map/psum | solution.py:149
  655.3 2.9 multiply_bitcast_fusion
  (270 shorter events, 118.2 us)
Async XLA Ops:
  7.2 56.5 %all-gather.4.cloned.1.call-start = ((), (), s32[]{:S(2)}) async-start(), calls=%async_computation.4 | async-start | bytes 2162688 | tf_op jit(solution)/shard_map/all_gather | solution.py:59
  7.9 165.9 %reduce-scatter.13.cloned.1.call-start = ((), (), s32[]{:S(2)}) async-start(), calls=%async_computation.9 | async-start | bytes 2359296
  8.7 58.9 %copy-start.16 = (s32[8,1,2]{2,0,1:T(8,128)}, s32[8,1,2]{2,0,1:T(8,128)S(1)}, u32[]{:S(2)}) copy-start(s32[8,1,2]{2,0,1:T(8,128)S(1)} %copy.96) | copy-start | bytes 196
  11.6 57.5 %copy-start.5 = (bf16[8,2,128,128]{3,2,1,0:T(8,128)(2,1)}, bf16[8,2,128,128]{3,2,1,0:T(8,128)(2,1)S(1)}, u32[]{:S(2)}) copy-start(bf16[8,2,128,128]{3,2,1,0:T(8,128)(2,1)S(1)} %get-tuple-element.952) | copy-start | bytes 1572868
  88.2 2.1 copy-start.6
  88.2 126.7 %copy-start.1 = (bf16[8,2,128,128]{3,2,1,0:T(8,128)(2,1)S(1)}, bf16[8,2,128,128]{3,2,1,0:T(8,128)(2,1)}, u32[]{:S(2)}) copy-start(bf16[8,2,128,128]{3,2,1,0:T(8,128)(2,1)} %get-tuple-element.920) | copy-start | bytes 1572868
  88.3 125.1 %all-gather.6.cloned.1.call-start = ((), (), s32[]{:S(2)}) async-start(), calls=%async_computation.5 | async-start | bytes 2359296 | tf_op jit(solution)/shard_map/all_gather | solution.py:81
  175.9 145.3 %reduce-scatter.9.cloned.1.call-start = ((), (), s32[]{:S(2)}) async-start(), calls=%async_computation.6 | async-start | bytes 2162688 | tf_op jit(solution)/shard_map/reduce_scatter | solution.py:92
  233.3 87.9 %copy-start.19 = (bf16[32,1024]{1,0:T(8,128)(2,1)S(1)}, bf16[32,1024]{1,0:T(8,128)(2,1)}, u32[]{:S(2)}) copy-start(bf16[32,1024]{1,0:T(8,128)(2,1)} %param.22) | copy-start | bytes 196612
  233.3 141.2 %all-gather.8.cloned.1.call-start = ((), (), s32[]{:S(2)}) async-start(), calls=%async_computation.7 | async-start | bytes 2162688 | tf_op jit(solution)/shard_map/all_gather | solution.py:99
  322.7 113.8 %reduce-scatter.15.cloned.1.call-start = ((), (), s32[]{:S(2)}) async-start(), calls=%async_computation.10 | async-start | bytes 2359296
  380.0 2.6 copy-start.2
  387.7 2.6 copy-start.2
  399.4 85.4 %copy-start.18 = (s32[8,1,2]{2,0,1:T(8,128)S(1)}, s32[8,1,2]{2,0,1:T(8,128)}, u32[]{:S(2)}) copy-start(s32[8,1,2]{2,0,1:T(8,128)} %get-tuple-element.1060) | copy-start | bytes 196
  399.4 258.8 %reduce-scatter.11.cloned.1.call-start = ((), (), s32[]{:S(2)}) async-start(), calls=%async_computation.8 | async-start | bytes 2162688 | tf_op jit(solution)/shard_map/reduce_scatter | solution.py:161
  438.0 6.5 collective-permute-start
  444.5 7.9 %collective-permute-start.1 = (bf16[128,1024]{0,1:T(8,128)(2,1)S(1)}, bf16[128,1024]{0,1:T(8,128)(2,1)S(1)}, u32[]{:S(2)}, u32[]{:S(2)}) collective-permute-start(bf16[128,1024]{0,1:T(8,128)(2,1)S(1)} %collective-permute-done), channel_id=1, source_target_pairs={{0,1},{1,2},{2,3},{3,4},{4,5},{5,6},{6,7},{7,0},{8,9},{9,10},{10,1... | collective-permute-start | bytes 786440 | tf_op jit(solution)/shard_map/ppermute | solution.py:119
  452.4 9.0 %collective-permute-start.2 = (bf16[128,1024]{0,1:T(8,128)(2,1)S(1)}, bf16[128,1024]{0,1:T(8,128)(2,1)S(1)}, u32[]{:S(2)}, u32[]{:S(2)}) collective-permute-start(bf16[128,1024]{0,1:T(8,128)(2,1)S(1)} %collective-permute-done.1), channel_id=1, source_target_pairs={{0,1},{1,2},{2,3},{3,4},{4,5},{5,6},{6,7},{7,0},{8,9},{9,10},{10,1... | collective-permute-start | bytes 786440 | tf_op jit(solution)/shard_map/ppermute | solution.py:119
  461.4 8.7 %collective-permute-start.3 = (bf16[128,1024]{0,1:T(8,128)(2,1)S(1)}, bf16[128,1024]{0,1:T(8,128)(2,1)S(1)}, u32[]{:S(2)}, u32[]{:S(2)}) collective-permute-start(bf16[128,1024]{0,1:T(8,128)(2,1)S(1)} %collective-permute-done.2), channel_id=1, source_target_pairs={{0,1},{1,2},{2,3},{3,4},{4,5},{5,6},{6,7},{7,0},{8,9},{9,10},{10,1... | collective-permute-start | bytes 786440 | tf_op jit(solution)/shard_map/ppermute | solution.py:119
  470.1 7.8 %collective-permute-start.4 = (bf16[128,1024]{0,1:T(8,128)(2,1)S(1)}, bf16[128,1024]{0,1:T(8,128)(2,1)S(1)}, u32[]{:S(2)}, u32[]{:S(2)}) collective-permute-start(bf16[128,1024]{0,1:T(8,128)(2,1)S(1)} %collective-permute-done.3), channel_id=1, source_target_pairs={{0,1},{1,2},{2,3},{3,4},{4,5},{5,6},{6,7},{7,0},{8,9},{9,10},{10,1... | collective-permute-start | bytes 786440 | tf_op jit(solution)/shard_map/ppermute | solution.py:119
  477.9 6.9 %collective-permute-start.5 = (bf16[128,1024]{0,1:T(8,128)(2,1)S(1)}, bf16[128,1024]{0,1:T(8,128)(2,1)S(1)}, u32[]{:S(2)}, u32[]{:S(2)}) collective-permute-start(bf16[128,1024]{0,1:T(8,128)(2,1)S(1)} %collective-permute-done.4), channel_id=1, source_target_pairs={{0,1},{1,2},{2,3},{3,4},{4,5},{5,6},{6,7},{7,0},{8,9},{9,10},{10,1... | collective-permute-start | bytes 786440 | tf_op jit(solution)/shard_map/ppermute | solution.py:119
  484.7 6.4 collective-permute-start.6
  494.3 1.6 copy-start.7
  521.6 2.6 copy-start
  521.6 2.6 copy-start.4
  533.3 3.0 copy-start
  533.3 3.0 copy-start.4
  546.6 3.0 copy-start
  546.6 3.0 copy-start.4
  560.0 3.0 copy-start
  560.0 3.0 copy-start.4
  565.7 88.6 %copy-start.8 = (f32[8,2,128,128]{2,3,1,0:T(8,128)S(1)}, f32[8,2,128,128]{2,3,1,0:T(8,128)}, u32[]{:S(2)}) copy-start(f32[8,2,128,128]{2,3,1,0:T(8,128)} %get-tuple-element.279) | copy-start | bytes 3145732
  (15 other events, 18.5 us)
Sparse Core Ops, SparseCore 0:
  10.6 53.0 all-gather.3
  88.4 37.1 reduce-scatter.12
  176.0 37.3 all-gather.5
  233.4 87.6 reduce-scatter.8
  324.1 50.3 all-gather.7
  399.5 36.9 reduce-scatter.14
  514.1 94.8 reduce-scatter.10
